TPU v7x, 32 devices: a whole 2x2x4 slice. The times are simulated.
32 devices in a mesh: seq: 8 (over z, y), grp: 4 (over x, core).
Axes of the slice: x: 2, y: 2, z: 4, core: 2. Of those that a mesh axis runs over, the one named last changes fastest.
Arguments:
- query_rows: bfloat16 [4096, 8192], P(('seq', 'grp')), may hold values from -6 to 6
- key_matrix: bfloat16 [4096, 1024], P(('seq', 'grp')), may hold values from -6 to 6
- value_matrix: bfloat16 [4096, 1024], P(('seq', 'grp')), may hold values from -6 to 6
- vertical: int32 [64, 3], replicated, may hold values from 0 to 63, as said below
- slash_offsets: int32 [64, 3], replicated, may hold values from 0 to 8, as said below
Outputs:
- attended: bfloat16 [4096, 8192], P(('seq', 'grp'))
Inputs may be any that keep to these rules, and one draw needn't show every extreme that they name: Each head's vertical blocks are distinct and rise along the row. `slash_offsets`: column 0 is 0; each head's offsets are distinct and rise along the row.
All inputs are finite; a program needn't handle non-finite values.
Results may differ from a plain program's by a relative error of at most 0.0043.
Values may be sent and summed in bfloat16 or wider, within the bound.
No kernel may reach another device: no remote copies, remote signals or barrier semaphores. Data moves between devices by JAX's collectives and lax.ppermute only.
A program may use at most 64 MiB of HBM per device.

v0:
```python
import jax
import jax.numpy as jnp
from jax import lax
from jax.sharding import PartitionSpec as P

HEAD_DIMENSION = 128
MASK_BLOCK_SIZE = 64


def passed_along(shard, axis, by):
    length = lax.axis_size(axis)
    pairs = [(i, i + by) for i in range(length) if 0 <= i + by < length]
    return lax.ppermute(shard, axis, pairs)


def head_attention(
    query_block, slash_keys, slash_values, vert_keys, vert_values, offsets, vert_blocks, first_block
):
    block_count, block_size, head_size = query_block.shape
    vert_tiled = jnp.broadcast_to(vert_keys[None], (block_count,) + vert_keys.shape)
    vert_vtiled = jnp.broadcast_to(vert_values[None], (block_count,) + vert_values.shape)
    all_keys = jnp.concatenate([slash_keys, vert_tiled], 1).reshape(block_count, -1, head_size)
    all_values = jnp.concatenate([slash_values, vert_vtiled], 1).reshape(block_count, -1, head_size)
    scores = jnp.einsum(
        "qid,qkd->qik", query_block, all_keys, preferred_element_type=jnp.float32
    ) * head_size ** (-0.5)
    query_index = first_block + jnp.arange(block_count, dtype=jnp.int32)
    slash_block = query_index[:, None] - offsets[None, :]
    slash_good = slash_block >= 0
    vert_good = (vert_blocks[None, :] <= query_index[:, None]) & jnp.all(
        query_index[:, None, None] - vert_blocks[None, :, None] != offsets[None, None, :], axis=2
    )
    block_ids = jnp.concatenate(
        [slash_block, jnp.broadcast_to(vert_blocks[None, :], (block_count, vert_blocks.shape[0]))],
        1,
    )
    block_good = jnp.concatenate([slash_good, vert_good], 1)
    position = jnp.arange(block_size, dtype=jnp.int32)
    key_pos = (block_ids[:, :, None] * block_size + position[None, None, :]).reshape(
        block_count, -1
    )
    query_pos = query_index[:, None] * block_size + position[None, :]
    allowed = jnp.repeat(block_good, block_size, axis=1)[:, None, :] & (
        key_pos[:, None, :] <= query_pos[:, :, None]
    )
    masked = jnp.where(allowed, scores, -1e30)
    row_top = jnp.max(masked, axis=2, keepdims=True)
    weight = jnp.where(allowed, jnp.exp(masked - row_top), 0.0)
    row_total = jnp.sum(weight, axis=2, keepdims=True)
    rounded = weight.astype(jnp.bfloat16)
    result = (
        jnp.einsum("qik,qkd->qid", rounded, all_values, preferred_element_type=jnp.float32)
        / row_total
    )
    return result.astype(jnp.bfloat16)


def per_device(query_rows, key_matrix, value_matrix, vertical, slash_offsets):
    tok_rows = query_rows.shape[0]
    grp_count = lax.axis_size("grp")
    head_size = HEAD_DIMENSION
    block_size = MASK_BLOCK_SIZE
    local_heads = query_rows.shape[1] // (grp_count * head_size)
    local_kv = key_matrix.shape[1] // (grp_count * head_size)
    group_sharing_factor = local_heads // local_kv
    query_split = query_rows.reshape(tok_rows, grp_count, local_heads * head_size)
    key_split = key_matrix.reshape(tok_rows, grp_count, local_kv * head_size)
    value_split = value_matrix.reshape(tok_rows, grp_count, local_kv * head_size)
    query_group, key_group, value_group = (
        lax.all_to_all(query_split, "grp", split_axis=1, concat_axis=0, tiled=True),
        lax.all_to_all(key_split, "grp", split_axis=1, concat_axis=0, tiled=True),
        lax.all_to_all(value_split, "grp", split_axis=1, concat_axis=0, tiled=True),
    )
    group_rows = tok_rows * grp_count
    group_blocks = group_rows // block_size
    key_local = key_group.reshape(group_rows, local_kv, head_size)
    value_local = value_group.reshape(group_rows, local_kv, head_size)
    key_before, value_before = passed_along((key_local, value_local), "seq", 1)
    key_window = (
        jnp.concatenate([key_before, key_local], 0)
        .reshape(2 * group_blocks, block_size, local_kv, head_size)
        .transpose(2, 0, 1, 3)
    )
    value_window = (
        jnp.concatenate([value_before, value_local], 0)
        .reshape(2 * group_blocks, block_size, local_kv, head_size)
        .transpose(2, 0, 1, 3)
    )
    seq_index = lax.axis_index("seq")
    grp_index = lax.axis_index("grp")
    head_offsets = lax.dynamic_slice_in_dim(slash_offsets, grp_index * local_heads, local_heads, 0)
    head_verts = lax.dynamic_slice_in_dim(vertical, grp_index * local_heads, local_heads, 0)
    kv_index = jnp.arange(local_heads, dtype=jnp.int32) // group_sharing_factor
    owner_seq = head_verts // group_blocks
    local_block = head_verts % group_blocks
    key_own = key_window[:, group_blocks:]
    value_own = value_window[:, group_blocks:]
    picked_keys = key_own[kv_index[:, None], local_block]
    picked_values = value_own[kv_index[:, None], local_block]
    owned = (owner_seq == seq_index)[:, :, None, None]
    nothing = jnp.zeros((), jnp.float32)
    summed_keys, summed_values = lax.psum(
        (
            jnp.where(owned, picked_keys.astype(jnp.float32), nothing),
            jnp.where(owned, picked_values.astype(jnp.float32), nothing),
        ),
        "seq",
    )
    vert_keys = summed_keys.astype(jnp.bfloat16)
    vert_values = summed_values.astype(jnp.bfloat16)
    head_queries = (
        query_group.reshape(group_rows, local_heads, head_size)
        .transpose(1, 0, 2)
        .reshape(local_heads, group_blocks, block_size, head_size)
    )
    nearby = jnp.arange(group_blocks, dtype=jnp.int32)
    first_block = seq_index * group_blocks

    def per_head(items):
        queries_one, offsets, vert_blocks, vert_key, vert_value, kv_one = items
        window_index = group_blocks + nearby[:, None] - offsets[None, :]
        slash_keys = key_window[kv_one][window_index]
        slash_values = value_window[kv_one][window_index]
        return head_attention(
            queries_one,
            slash_keys,
            slash_values,
            vert_key,
            vert_value,
            offsets,
            vert_blocks,
            first_block,
        )

    results = lax.map(
        per_head, (head_queries, head_offsets, head_verts, vert_keys, vert_values, kv_index)
    )
    merged = (
        results.reshape(local_heads, group_rows, head_size)
        .transpose(1, 0, 2)
        .reshape(group_rows, 1, local_heads * head_size)
    )
    returned = lax.all_to_all(merged, "grp", split_axis=0, concat_axis=1, tiled=True)
    return returned.reshape(tok_rows, grp_count * local_heads * head_size)


def solution(mesh):
    return jax.shard_map(
        per_device,
        mesh=mesh,
        in_specs=(
            P(("seq", "grp"), None),
            P(("seq", "grp"), None),
            P(("seq", "grp"), None),
            P(),
            P(),
        ),
        out_specs=P(("seq", "grp"), None),
        check_vma=False,
    )
```

profile of v0, /device:TPU:0, one launch (start us, length us, event | category | flops | bytes accessed | tf_op | source)
XLA Modules:
  0.0 408.5 jit_solution(12489217705326246221)
XLA Ops:
  0.0 1.8 copy.79
  1.8 4.2 %all-to-all-start.2 = ((bf16[128,4,256]{2,0,1:T(8,128)(2,1)}), bf16[128,4,256]{2,0,1:T(8,128)(2,1)S(1)}, u32[]{:S(2)}, u32[]{:S(2)}) async-start(bf16[128,4,256]{2,0,1:T(8,128)(2,1)} %bitcast.88), calls=%async_computation.2 | async-start | bytes 524288 | tf_op jit(solution)/shard_map/all_to_all | solution.py:72
  6.3 1.7 copy.80
  8.0 4.1 all-to-all-done.2
  12.1 3.4 all-to-all-start.1
  15.6 4.1 collective-permute-start.1
  21.5 3.7 all-to-all-start
  25.3 4.1 collective-permute-start
  30.4 5.1 %collective-permute-done = bf16[512,2,128]{2,1,0:T(2,128)(2,1)S(1)} collective-permute-done((bf16[512,2,128]{2,1,0:T(2,128)(2,1)S(1)}, bf16[512,2,128]{2,1,0:T(2,128)(2,1)S(1)}, u32[]{:S(2)}, u32[]{:S(2)}) %collective-permute-start) | collective-permute-done | bytes 262176 | tf_op jit(solution)/shard_map/ppermute | solution.py:13
  37.3 1.8 gather_fusion.2
  39.1 1.8 gather_fusion.3
  40.9 3.3 convert_select_fusion
  44.3 128.2 %all-reduce.2 = (bf16[16,3,64,128]{3,2,1,0:T(8,128)(2,1)}, bf16[16,3,64,128]{3,2,1,0:T(8,128)(2,1)}) all-reduce(f32[16,3,64,128]{3,2,1,0:T(8,128)} %get-tuple-element.173, f32[16,3,64,128]{3,2,1,0:T(8,128)} %get-tuple-element.172), channel_id=1, replica_groups=mesh['seq'=8,'grp'=4] {'seq'}, use_global_device_ids=true, to_apply=%region_0.1 | all-reduce | flops 786432 | bytes 4718592 | tf_op jit(solution)/shard_map/psum | solution.py:102
  173.1 1.9 copy.61
  175.0 178.8 %while.11 = (s32[]{:T(128)}, bf16[16,8,64,128]{3,2,1,0:T(8,128)(2,1)}, s32[]{:T(128)}, s32[16,3]{1,0:T(8,128)S(1)}, s32[16,3]{1,0:T(8,128)S(1)}, /*index=5*/bf16...) while((s32[]{:T(128)}, ...), condition=%wide.region_6.7_spmd.clone, body=%wide.region_2.6_spmd.clone.sunk | while | flops 104339728 | bytes 11976439 | solution.py:135
  353.8 2.9 copy.62
  357.2 2.9 reduce
  360.1 2.9 copy.81
  363.0 2.8 reshape.314
  365.8 29.3 %all_to_all.60 = bf16[4,2,131072]{2,1,0:T(2,128)(2,1)S(1)} all-to-all(bf16[4,2,131072]{2,1,0:T(2,128)(2,1)} %reshape.314), channel_id=1, replica_groups=mesh['seq'=8,'grp'=4] {'grp'}, dimensions={0} | all-to-all | bytes 4194304 | tf_op jit(solution)/shard_map/all_to_all | solution.py:143
  395.1 3.3 reshape.315
  398.4 3.5 copy.66
  401.9 2.6 copy.64
  404.4 4.1 copy.65
  (578 shorter events, 153.9 us)
Async XLA Ops:
  0.0 6.0 %copy-start = (s32[64,3]{0,1:T(4,128)S(1)}, s32[64,3]{0,1:T(4,128)}, u32[]{:S(2)}) copy-start(s32[64,3]{0,1:T(4,128)} %param.10) | copy-start | bytes 2308
  0.0 19.6 %copy-start.2 = (bf16[128,8192]{1,0:T(8,128)(2,1)S(1)}, bf16[128,8192]{1,0:T(8,128)(2,1)}, u32[]{:S(2)}) copy-start(bf16[128,8192]{1,0:T(8,128)(2,1)} %param.7) | copy-start | bytes 6291460
  1.8 10.2 %all-to-all-start.2 = ((bf16[128,4,256]{2,0,1:T(8,128)(2,1)}), bf16[128,4,256]{2,0,1:T(8,128)(2,1)S(1)}, u32[]{:S(2)}, u32[]{:S(2)}) async-start(bf16[128,4,256]{2,0,1:T(8,128)(2,1)} %bitcast.88), calls=%async_computation.2 | async-start | bytes 524288 | tf_op jit(solution)/shard_map/all_to_all | solution.py:72
  12.1 9.4 %all-to-all-start.1 = ((bf16[128,4,256]{2,0,1:T(8,128)(2,1)}), bf16[128,4,256]{2,0,1:T(8,128)(2,1)S(1)}, u32[]{:S(2)}, u32[]{:S(2)}) async-start(bf16[128,4,256]{2,0,1:T(8,128)(2,1)} %bitcast.89), calls=%async_computation.1 | async-start | bytes 524288 | tf_op jit(solution)/shard_map/all_to_all | solution.py:71
  15.6 14.2 %collective-permute-start.1 = (bf16[512,2,128]{2,1,0:T(2,128)(2,1)S(1)}, bf16[512,2,128]{2,1,0:T(2,128)(2,1)S(1)}, u32[]{:S(2)}, u32[]{:S(2)}) collective-permute-start(bf16[512,2,128]{2,1,0:T(2,128)(2,1)S(1)} %reshape.263), channel_id=1, source_target_pairs={{0,4},{4,8},{8,12},{12,16},{16,20},{20,24},{24,28},{1,5},{5,9},{9,... | collective-permute-start | bytes 786440 | tf_op jit(solution)/shard_map/ppermute | solution.py:13
  21.5 7.9 %copy-start.3 = (s32[64,3]{0,1:T(4,128)S(1)}, s32[64,3]{0,1:T(4,128)}, u32[]{:S(2)}) copy-start(s32[64,3]{0,1:T(4,128)} %param.11) | copy-start | bytes 2308
  21.5 151.0 %all-to-all-start = ((bf16[128,4,2048]{2,0,1:T(8,128)(2,1)}), bf16[128,4,2048]{2,0,1:T(8,128)(2,1)S(1)}, u32[]{:S(2)}, u32[]{:S(2)}) async-start(bf16[128,4,2048]{2,0,1:T(8,128)(2,1)} %bitcast.87), calls=%async_computation | async-start | bytes 4194304 | tf_op jit(solution)/shard_map/all_to_all | solution.py:70
  25.3 10.2 %collective-permute-start = (bf16[512,2,128]{2,1,0:T(2,128)(2,1)S(1)}, bf16[512,2,128]{2,1,0:T(2,128)(2,1)S(1)}, u32[]{:S(2)}, u32[]{:S(2)}) collective-permute-start(bf16[512,2,128]{2,1,0:T(2,128)(2,1)S(1)} %reshape.260), channel_id=1, source_target_pairs={{0,4},{4,8},{8,12},{12,16},{16,20},{20,24},{24,28},{1,5},{5,9},{9,... | collective-permute-start | bytes 786440 | tf_op jit(solution)/shard_map/ppermute | solution.py:13
  36.5 0.8 copy-start.1
where the time goes:
time: 411 us; the launch traced here: 408 us
  blocking collectives  157 us (38%)
  local copies, waits for them, and re-layouts  109 us (27%)
  matrix products  48.8 us (12%)
  other arithmetic  33 us (8%)
  loops' own time  31.1 us (8%)
  starting transfers between devices  19.5 us (5%)
  waiting for transfers between devices  9.59 us (2%)
    psum x1, blocking collectives, per_device(): lax.psum((jnp.where(owned, picked_keys.astype(jnp.float32), nothing), jnp...  128 us
    another operation x1, loops' own time, per_device(): lax.map(per_head, (head_queries, head_offsets, head_verts, vert_keys, ver...  31.1 us
    all_to_all x1, blocking collectives, per_device(): lax.all_to_all(merged, 'grp', split_axis=0, concat_axis=1, tiled=True)  29.3 us
    dot_general x16, matrix products, head_attention(): jnp.einsum('qik,qkd->qid', rounded, all_values, preferred_element_type=jn...  26.6 us
    dot_general x16, matrix products, head_attention(): jnp.einsum('qid,qkd->qik', query_block, all_keys, preferred_element_type=...  22.1 us
    squeeze x16, local copies, waits for them, and re-layouts, per_head(): slash_values = value_window[kv_one][window_index]  16.3 us
    sub x16, other arithmetic, head_attention(): weight = jnp.where(allowed, jnp.exp(masked - row_top), 0.0)  16.2 us
    unnamed x16, local copies, waits for them, and re-layouts  16 us
  transfers between devices with their start and end apart: 5, of which 3 were waited for; matrix products, arithmetic and copies ran while one was open for 3% of the time, Pallas kernels for 0%

commit v1 on v0

--- a/solution.py
+++ b/solution.py
@@ -140,7 +140,22 @@
         .transpose(1, 0, 2)
         .reshape(group_rows, 1, local_heads * head_size)
     )
-    returned = lax.all_to_all(merged, "grp", split_axis=0, concat_axis=1, tiled=True)
+    w_next = lax.axis_index("grp")
+    e_now = lax.axis_size("grp")
+    value_now, tmp = (e_now, w_next)
+    taken_in = merged.shape[0] // value_now
+    response = list(merged.shape)
+    response[0] = taken_in
+    carry_in = response[1]
+    response[1] = carry_in * value_now
+    returned = jnp.zeros(response, merged.dtype)
+    s = 0
+    while s < value_now:
+        u1 = lax.dynamic_slice_in_dim(merged, (tmp ^ s) * taken_in, taken_in, axis=0)
+        if s:
+            u1 = lax.ppermute(u1, "grp", [(ix, ix ^ s) for ix in range(value_now)])
+        returned = lax.dynamic_update_slice_in_dim(returned, u1, (tmp ^ s) * carry_in, axis=1)
+        s += 1
     return returned.reshape(tok_rows, grp_count * local_heads * head_size)
 
 

time: 411 us -> 395 us (0.961)
  blocking collectives: 157 us -> 128 us
  waiting for transfers between devices: 9.59 us -> 28 us
    all_to_all x1 -> x0, blocking collectives: 29.3 us -> none  [per_device(): lax.all_to_all(merged, 'grp', split_axis=0, concat_axis=1, tiled=True)]
    ppermute x0 -> x3, waiting for transfers between devices: none -> 18.4 us  [per_device(): u1 = lax.ppermute(u1, 'grp', [(ix, ix ^ s) for ix in range(value_now)])]
    dynamic_update_slice x0 -> x4, local copies, waits for them, and re-layouts: none -> 11.5 us  [per_device(): lax.dynamic_update_slice_in_dim(returned, u1, (tmp ^ s) * carry_in, axis=1)]
    unnamed x16 -> x15, local copies, waits for them, and re-layouts: 16 us -> 7.53 us
    reshape x2 -> x0, local copies, waits for them, and re-layouts: 4.59 us -> none  [the longest x1 4.06 us: per_device(): return returned.reshape(tok_rows, grp_count * local_heads * head_size)]
  transfers between devices with their start and end apart: 5 -> 8, of which waited for: 3 -> 6; matrix products, arithmetic and copies ran while one was open for 3% -> 4% of each run, Pallas kernels for 0% -> 0%
where the time goes in v1:
time: 395 us; the launch traced here: 392 us
  blocking collectives  128 us (32%)
  local copies, waits for them, and re-layouts  108 us (27%)
  matrix products  48.8 us (12%)
  other arithmetic  30.1 us (8%)
  waiting for transfers between devices  28 us (7%)
  loops' own time  27.5 us (7%)
  starting transfers between devices  21.3 us (5%)
    psum x1, blocking collectives, per_device(): lax.psum((jnp.where(owned, picked_keys.astype(jnp.float32), nothing), jnp...  128 us
    another operation x1, loops' own time, per_device(): lax.map(per_head, (head_queries, head_offsets, head_verts, vert_keys, ver...  27.5 us
    dot_general x16, matrix products, head_attention(): jnp.einsum('qik,qkd->qid', rounded, all_values, preferred_element_type=jn...  26.6 us
    dot_general x16, matrix products, head_attention(): jnp.einsum('qid,qkd->qik', query_block, all_keys, preferred_element_type=...  22.1 us
    ppermute x3, waiting for transfers between devices, per_device(): u1 = lax.ppermute(u1, 'grp', [(ix, ix ^ s) for ix in range(value_now)])  18.4 us
    squeeze x16, local copies, waits for them, and re-layouts, per_head(): slash_values = value_window[kv_one][window_index]  16.3 us
    sub x16, other arithmetic, head_attention(): weight = jnp.where(allowed, jnp.exp(masked - row_top), 0.0)  16.2 us
    broadcast_in_dim x32, local copies, waits for them, and re-layouts, head_attention(): jnp.broadcast_to(vert_values[None], (block_count,) + vert_values.shape)  14.6 us
  transfers between devices with their start and end apart: 8, of which 6 were waited for; matrix products, arithmetic and copies ran while one was open for 4% of the time, Pallas kernels for 0%

profile of v1, /device:TPU:0, one launch (start us, length us, event | category | flops | bytes accessed | tf_op | source)
XLA Modules:
  0.0 392.1 jit_solution(13412131333629569536)
XLA Ops:
  0.0 1.8 copy.65
  1.8 4.2 %all-to-all-start.2 = ((bf16[128,4,256]{2,0,1:T(8,128)(2,1)}), bf16[128,4,256]{2,0,1:T(8,128)(2,1)S(1)}, u32[]{:S(2)}, u32[]{:S(2)}) async-start(bf16[128,4,256]{2,0,1:T(8,128)(2,1)} %bitcast.86), calls=%async_computation.2 | async-start | bytes 524288 | tf_op jit(solution)/shard_map/all_to_all | solution.py:72
  8.0 4.1 %all-to-all-done.2 = bf16[128,4,256]{2,0,1:T(8,128)(2,1)S(1)} async-done(((bf16[128,4,256]{2,0,1:T(8,128)(2,1)}), bf16[128,4,256]{2,0,1:T(8,128)(2,1)S(1)}, u32[]{:S(2)}, u32[]{:S(2)}) %all-to-all-start.2) | async-done | bytes 262176 | tf_op jit(solution)/shard_map/all_to_all | solution.py:72
  12.1 3.4 all-to-all-start.1
  15.6 4.1 %collective-permute-start.1 = (bf16[512,2,128]{2,1,0:T(2,128)(2,1)S(1)}, bf16[512,2,128]{2,1,0:T(2,128)(2,1)S(1)}, u32[]{:S(2)}, u32[]{:S(2)}) collective-permute-start(bf16[512,2,128]{2,1,0:T(2,128)(2,1)S(1)} %reshape.262), channel_id=1, source_target_pairs={{0,4},{4,8},{8,12},{12,16},{16,20},{20,24},{24,28},{1,5},{5,9},{9,... | collective-permute-start | bytes 786440 | tf_op jit(solution)/shard_map/ppermute | solution.py:13
  21.5 3.7 all-to-all-start
  25.3 4.1 %collective-permute-start = (bf16[512,2,128]{2,1,0:T(2,128)(2,1)S(1)}, bf16[512,2,128]{2,1,0:T(2,128)(2,1)S(1)}, u32[]{:S(2)}, u32[]{:S(2)}) collective-permute-start(bf16[512,2,128]{2,1,0:T(2,128)(2,1)S(1)} %reshape.259), channel_id=1, source_target_pairs={{0,4},{4,8},{8,12},{12,16},{16,20},{20,24},{24,28},{1,5},{5,9},{9,... | collective-permute-start | bytes 786440 | tf_op jit(solution)/shard_map/ppermute | solution.py:13
  30.4 5.1 %collective-permute-done = bf16[512,2,128]{2,1,0:T(2,128)(2,1)S(1)} collective-permute-done((bf16[512,2,128]{2,1,0:T(2,128)(2,1)S(1)}, bf16[512,2,128]{2,1,0:T(2,128)(2,1)S(1)}, u32[]{:S(2)}, u32[]{:S(2)}) %collective-permute-start) | collective-permute-done | bytes 262176 | tf_op jit(solution)/shard_map/ppermute | solution.py:13
  37.3 1.8 gather_fusion.2
  39.1 1.8 gather_fusion.3
  40.9 3.3 convert_select_fusion
  44.2 128.2 %all-reduce.2 = (bf16[16,3,64,128]{3,2,1,0:T(8,128)(2,1)}, bf16[16,3,64,128]{3,2,1,0:T(8,128)(2,1)}) all-reduce(f32[16,3,64,128]{3,2,1,0:T(8,128)} %get-tuple-element.166, f32[16,3,64,128]{3,2,1,0:T(8,128)} %get-tuple-element.165), channel_id=1, replica_groups=mesh['seq'=8,'grp'=4] {'seq'}, use_global_device_ids=true, to_apply=%region_0.1 | all-reduce | flops 786432 | bytes 4718592 | tf_op jit(solution)/shard_map/psum | solution.py:102
  173.1 1.9 copy.48
  175.0 174.6 %while.11 = (s32[]{:T(128)}, bf16[16,8,64,128]{3,2,1,0:T(8,128)(2,1)}, s32[]{:T(128)}, s32[16,3]{1,0:T(8,128)S(1)}, s32[16,3]{1,0:T(8,128)S(1)}, /*index=5*/bf16...) while((s32[]{:T(128)}, ...), condition=%wide.region_6.7_spmd.clone, body=%wide.region_2.6_spmd.clone.sunk | while | flops 104339728 | bytes 11976439 | solution.py:135
  206.0 1.7 fusion.49
  271.5 1.7 fusion.49
  304.2 1.7 fusion.49
  349.5 2.9 copy.49
  358.1 11.8 %collective-permute-done.3 = bf16[128,1,2048]{0,2,1:T(8,128)(2,1)S(1)} collective-permute-done((bf16[128,1,2048]{0,2,1:T(8,128)(2,1)S(1)}, bf16[128,1,2048]{0,2,1:T(8,128)(2,1)S(1)}, u32[]{:S(2)}, u32[]{:S(2)}) %collective-permute-start.3) | collective-permute-done | bytes 524320 | tf_op jit(solution)/shard_map/ppermute | solution.py:156
  370.7 3.4 copy.50
  374.2 6.3 %collective-permute-done.4 = bf16[128,1,2048]{0,2,1:T(8,128)(2,1)} collective-permute-done((bf16[128,1,2048]{0,2,1:T(8,128)(2,1)S(1)}, bf16[128,1,2048]{0,2,1:T(8,128)(2,1)}, u32[]{:S(2)}, u32[]{:S(2)}) %collective-permute-start.4) | collective-permute-done | bytes 524320 | tf_op jit(solution)/shard_map/ppermute | solution.py:156
  380.5 2.5 copy.51
  383.0 6.4 %dynamic_update_slice.19 = bf16[128,4,2048]{2,1,0:T(4,128)(2,1)S(1)} dynamic-update-slice(bf16[128,4,2048]{2,1,0:T(4,128)(2,1)S(1)} %copy.50, bf16[128,1,2048]{2,1,0:T(2,128)(2,1)S(1)} %copy.51, s32[]{:T(128)} %constant.94.clone.1, s32[]{:T(128)S(6)} %select_n.108, s32[]{:T(128)} %constant.94.clone.1) | dynamic-update-slice | bytes 1048580 | tf_op jit(solution)/shard_map/dynamic_update_slice | solution.py:157
  389.4 2.7 copy.58
  (585 shorter events, 155.9 us)
Async XLA Ops:
  0.0 6.0 %copy-start = (s32[64,3]{0,1:T(4,128)S(1)}, s32[64,3]{0,1:T(4,128)}, u32[]{:S(2)}) copy-start(s32[64,3]{0,1:T(4,128)} %param.10) | copy-start | bytes 2308
  0.0 19.6 %copy-start.3 = (bf16[128,8192]{1,0:T(8,128)(2,1)S(1)}, bf16[128,8192]{1,0:T(8,128)(2,1)}, u32[]{:S(2)}) copy-start(bf16[128,8192]{1,0:T(8,128)(2,1)} %param.7) | copy-start | bytes 6291460
  1.8 10.2 %all-to-all-start.2 = ((bf16[128,4,256]{2,0,1:T(8,128)(2,1)}), bf16[128,4,256]{2,0,1:T(8,128)(2,1)S(1)}, u32[]{:S(2)}, u32[]{:S(2)}) async-start(bf16[128,4,256]{2,0,1:T(8,128)(2,1)} %bitcast.86), calls=%async_computation.2 | async-start | bytes 524288 | tf_op jit(solution)/shard_map/all_to_all | solution.py:72
  12.1 9.4 %all-to-all-start.1 = ((bf16[128,4,256]{2,0,1:T(8,128)(2,1)}), bf16[128,4,256]{2,0,1:T(8,128)(2,1)S(1)}, u32[]{:S(2)}, u32[]{:S(2)}) async-start(bf16[128,4,256]{2,0,1:T(8,128)(2,1)} %bitcast.87), calls=%async_computation.1 | async-start | bytes 524288 | tf_op jit(solution)/shard_map/all_to_all | solution.py:71
  15.6 14.2 %collective-permute-start.1 = (bf16[512,2,128]{2,1,0:T(2,128)(2,1)S(1)}, bf16[512,2,128]{2,1,0:T(2,128)(2,1)S(1)}, u32[]{:S(2)}, u32[]{:S(2)}) collective-permute-start(bf16[512,2,128]{2,1,0:T(2,128)(2,1)S(1)} %reshape.262), channel_id=1, source_target_pairs={{0,4},{4,8},{8,12},{12,16},{16,20},{20,24},{24,28},{1,5},{5,9},{9,... | collective-permute-start | bytes 786440 | tf_op jit(solution)/shard_map/ppermute | solution.py:13
  21.5 7.9 %copy-start.4 = (s32[64,3]{0,1:T(4,128)S(1)}, s32[64,3]{0,1:T(4,128)}, u32[]{:S(2)}) copy-start(s32[64,3]{0,1:T(4,128)} %param.11) | copy-start | bytes 2308
  21.5 151.0 %all-to-all-start = ((bf16[128,4,2048]{2,0,1:T(8,128)(2,1)}), bf16[128,4,2048]{2,0,1:T(8,128)(2,1)S(1)}, u32[]{:S(2)}, u32[]{:S(2)}) async-start(bf16[128,4,2048]{2,0,1:T(8,128)(2,1)} %bitcast.85), calls=%async_computation | async-start | bytes 4194304 | tf_op jit(solution)/shard_map/all_to_all | solution.py:70
  25.3 10.2 %collective-permute-start = (bf16[512,2,128]{2,1,0:T(2,128)(2,1)S(1)}, bf16[512,2,128]{2,1,0:T(2,128)(2,1)S(1)}, u32[]{:S(2)}, u32[]{:S(2)}) collective-permute-start(bf16[512,2,128]{2,1,0:T(2,128)(2,1)S(1)} %reshape.259), channel_id=1, source_target_pairs={{0,4},{4,8},{8,12},{12,16},{16,20},{20,24},{24,28},{1,5},{5,9},{9,... | collective-permute-start | bytes 786440 | tf_op jit(solution)/shard_map/ppermute | solution.py:13
  36.5 0.8 copy-start.2
  353.9 1.3 copy-start.1
  355.2 2.1 collective-permute-start.2
  355.2 14.7 %collective-permute-start.3 = (bf16[128,1,2048]{0,2,1:T(8,128)(2,1)S(1)}, bf16[128,1,2048]{0,2,1:T(8,128)(2,1)S(1)}, u32[]{:S(2)}, u32[]{:S(2)}) collective-permute-start(bf16[128,1,2048]{0,2,1:T(8,128)(2,1)S(1)} %get-tuple-element.162), channel_id=1, source_target_pairs={{0,2},{1,3},{2,0},{3,1},{4,6},{5,7},{6,4},{7,5},{8,10},{9,11},{10,... | collective-permute-start | bytes 1572872 | tf_op jit(solution)/shard_map/ppermute | solution.py:156
  356.4 24.0 %collective-permute-start.4 = (bf16[128,1,2048]{0,2,1:T(8,128)(2,1)S(1)}, bf16[128,1,2048]{0,2,1:T(8,128)(2,1)}, u32[]{:S(2)}, u32[]{:S(2)}) collective-permute-start(bf16[128,1,2048]{0,2,1:T(8,128)(2,1)S(1)} %get-tuple-element.161), channel_id=1, source_target_pairs={{0,3},{1,2},{2,1},{3,0},{4,7},{5,6},{6,5},{7,4},{8,11},{9,10},{10,... | collective-permute-start | bytes 1572872 | tf_op jit(solution)/shard_map/ppermute | solution.py:156
